TPU v7x, 256 devices: a whole 4x4x8 slice. The times are simulated.
256 devices in a mesh: member: 4 (over z_hi), token: 64 (over z_lo, x, y, core).
Axes of the slice: x: 4, y: 4, z: 8 (z_hi: 4, z_lo: 2; z = z_hi * 2 + z_lo), core: 2. Of those that a mesh axis runs over, the one named last changes fastest.
Arguments:
- members_in: bfloat16 [8, 8192, 1024], P('member', 'token'), may hold values from -16 to 16
- member_noise: bfloat16 [8, 8192, 1024], P('member', 'token'), may hold values from -6 to 6
- norm_gain: float32 [1024], replicated, may hold values from 0.25 to 1.75
- weight_query: bfloat16 [1024, 1024], replicated, may hold values from -0.1875 to 0.1875
- weight_key: bfloat16 [1024, 1024], replicated, may hold values from -0.1875 to 0.1875
- weight_value: bfloat16 [1024, 1024], replicated, may hold values from -0.1875 to 0.1875
- weight_out: bfloat16 [1024, 1024], replicated, may hold values from -0.1875 to 0.1875
- decoder_projection_weight: bfloat16 [100, 1024], replicated, may hold values from -0.1875 to 0.1875
- decoder_bias: float32 [100], replicated, may hold values from -3 to 3
- observations: float32 [100, 65536], P(None, 'token'), may hold values from -6 to 6
- surface_extent_factor: float32 [65536], P('token'), may hold values from 0.3 to 3
- quantity_scoring_factor: float32 [100], replicated, may hold values from 0.2 to 2
- point_map: int32 [65536], P('token'), may hold values from 0 to 127
Outputs:
- mean_scoring: float32 [], replicated
- grad_members: bfloat16 [8, 8192, 1024], P('member', 'token')
- grad_out: float32 [1024, 1024], P('token')
- grad_decoder: float32 [100, 1024], replicated
Inputs may be any that keep to these rules, and one draw needn't show every extreme that they name: Point p belongs to token (p // 1024) * 128 + point_map[p].
All inputs are finite; a program needn't handle non-finite values.
Results may differ from a plain program's by a relative error of at most 0.015.
Values may be sent and summed in bfloat16 or wider, within the bound.
No kernel may reach another device: no remote copies, remote signals or barrier semaphores. Data moves between devices by JAX's collectives and lax.ppermute only.
A program may use at most 128 MiB of HBM per device.

v0:
```python
import jax
import jax.numpy as jnp
from jax import lax
from jax.sharding import PartitionSpec as P

HEADS = 16
HALF = 128
EPSILON = 1e-06
SMOOTH = 0.01


def extended_2(block, sides, width):
    for axis, dim in sides:
        count = lax.axis_size(axis)
        forward = [(i, i + 1) for i in range(count - 1)]
        backward = [(target, source) for source, target in forward]
        low = lax.ppermute(
            lax.slice_in_dim(block, block.shape[dim] - width, None, axis=dim), axis, forward
        )
        high = lax.ppermute(lax.slice_in_dim(block, 0, width, axis=dim), axis, backward)
        block = jnp.concatenate([low, block, high], axis=dim)
    return block


def from_behind(block, axis, distance):
    devices = range(lax.axis_size(axis))
    route = [(i - distance, i) for i in devices if i - distance in devices]
    return lax.ppermute(block, axis, route)


def normalize_heads(flat):
    rows, width = flat.shape
    split = flat.reshape(rows, HEADS, width // HEADS)
    split = split * lax.rsqrt(jnp.mean(split * split, axis=-1, keepdims=True) + EPSILON)
    return split.reshape(rows, width)


def project(state_in, member_noise, norm_gain, weight_query, weight_key, weight_value):
    member_rows, tokens, width = state_in.shape
    mixed = state_in + member_noise.astype(jnp.float32)
    normed = (
        mixed * lax.rsqrt(jnp.mean(mixed * mixed, axis=-1, keepdims=True) + EPSILON) * norm_gain
    ).astype(jnp.bfloat16)
    flat = normed.reshape(member_rows * tokens, width)
    query = normalize_heads(jnp.dot(flat, weight_query, preferred_element_type=jnp.float32)).astype(
        jnp.bfloat16
    )
    key = normalize_heads(jnp.dot(flat, weight_key, preferred_element_type=jnp.float32)).astype(
        jnp.bfloat16
    )
    value = jnp.dot(flat, weight_value, preferred_element_type=jnp.float32).astype(jnp.bfloat16)
    full_shape = (member_rows, tokens, width)
    return (query.reshape(full_shape), key.reshape(full_shape), value.reshape(full_shape))


def attend(query, keys, values, leading_realization, total):
    member_rows, queries, width = query.shape
    realization_number = keys.shape[1]
    depth = width // HEADS
    query_heads = query.reshape(member_rows, queries, HEADS, depth)
    key_heads = keys.reshape(member_rows, realization_number, HEADS, depth)
    value_heads = values.reshape(member_rows, realization_number, HEADS, depth)
    scores = jnp.einsum(
        "mqhd,mkhd->mhqk", query_heads, key_heads, preferred_element_type=jnp.float32
    ) / jnp.sqrt(jnp.float32(depth))
    query_pos = leading_realization + lax.iota(jnp.int32, queries)
    key_pos = leading_realization - HALF + lax.iota(jnp.int32, realization_number)
    allowed = (key_pos[None, :] >= query_pos[:, None] - HALF) & (
        key_pos[None, :] < query_pos[:, None] + HALF
    )
    allowed = allowed & (key_pos[None, :] >= 0) & (key_pos[None, :] < total)
    raised = jnp.where(allowed[None, None], jnp.exp(scores), jnp.float32(0.0))
    probs = (raised / jnp.sum(raised, axis=-1, keepdims=True)).astype(jnp.bfloat16)
    mixed = jnp.einsum("mhqk,mkhd->mqhd", probs, value_heads, preferred_element_type=jnp.float32)
    return mixed.reshape(member_rows, queries, width).astype(jnp.bfloat16)


def softened_magnitude(diff):
    return jnp.sqrt(diff * diff + SMOOTH)


def unbiased_ranked_score(
    realization_prediction, observed_grid, surface_extent, quantity_scoring_factor
):
    realization_number = realization_prediction.shape[0]
    accuracy_part = softened_magnitude(realization_prediction[0] - observed_grid)
    for realization_position in range(1, realization_number):
        accuracy_part = accuracy_part + softened_magnitude(
            realization_prediction[realization_position] - observed_grid
        )
    dispersion_part = jnp.zeros_like(accuracy_part)
    for leading_realization in range(realization_number):
        for paired_realization in range(leading_realization + 1, realization_number):
            dispersion_part = dispersion_part + softened_magnitude(
                realization_prediction[leading_realization]
                - realization_prediction[paired_realization]
            )
    score = accuracy_part / realization_number - dispersion_part / (
        realization_number * (realization_number - 1)
    )
    return jnp.sum(quantity_scoring_factor[:, None] * surface_extent[None, :] * score)


def shards(
    members_in,
    member_noise,
    norm_gain,
    weight_query,
    weight_key,
    weight_value,
    weight_out,
    decoder_projection_weight,
    decoder_bias,
    observations,
    surface_extent_factor,
    quantity_scoring_factor,
    point_map,
):
    member_rows, tokens, width = members_in.shape
    state = members_in.astype(jnp.float32)

    def front(state_in):
        return project(state_in, member_noise, norm_gain, weight_query, weight_key, weight_value)

    (query, key, value), front_pull = jax.vjp(front, state)
    stacked = jnp.stack([key, value])
    extended = extended_2(stacked, (("token", 2),), HALF)
    leading_realization = lax.axis_index("token") * tokens
    total = tokens * lax.axis_size("token")

    def middle(query_in, extended_in):
        return attend(query_in, extended_in[0], extended_in[1], leading_realization, total)

    attended, middle_pull = jax.vjp(middle, query, extended)
    flat_att = attended.reshape(member_rows * tokens, width)
    update = jnp.dot(flat_att, weight_out, preferred_element_type=jnp.float32).reshape(
        member_rows, tokens, width
    )
    residual_stream_state = (state + member_noise.astype(jnp.float32) + update).astype(jnp.bfloat16)

    def decode_tokens(residual_in, decoder_in):
        mapping_array = jnp.einsum(
            "vc,mtc->mvt",
            decoder_in.astype(jnp.bfloat16),
            residual_in,
            preferred_element_type=jnp.float32,
        )
        mapping_array = mapping_array + decoder_bias[None, :, None]
        return jnp.take(mapping_array, point_map, axis=2)

    realization_prediction, readout_slope_pulled = jax.vjp(
        decode_tokens, residual_stream_state, decoder_projection_weight.astype(jnp.float32)
    )
    location_places = realization_prediction.shape[2]
    groups = lax.axis_size("member")
    local_shard = lax.axis_index("member")
    gathered_lines = lax.all_gather(realization_prediction, "member", axis=0, tiled=True)

    def score_all(whole):
        return unbiased_ranked_score(
            whole, observations, surface_extent_factor, quantity_scoring_factor
        )

    full_loss, score_pull = jax.vjp(score_all, gathered_lines)
    (complete_gradient,) = score_pull(jnp.ones((), jnp.float32))
    prediction_slope = lax.dynamic_slice_in_dim(
        complete_gradient, local_shard * member_rows, member_rows, 0
    )
    partial_loss = full_loss / groups
    carried_slope, readout_piece_result = readout_slope_pulled(prediction_slope)
    overall_scoring_amount, grad_decoder = lax.psum(
        (partial_loss, readout_piece_result), ("member", "token")
    )
    mean_scoring = overall_scoring_amount / (
        realization_prediction.shape[1] * location_places * lax.axis_size("token")
    )
    flat_grad = carried_slope.reshape(member_rows * tokens, width)
    grad_attended = (
        jnp.dot(flat_grad, weight_out.T, preferred_element_type=jnp.float32)
        .astype(jnp.bfloat16)
        .reshape(member_rows, tokens, width)
    )
    grad_query, grad_extended = middle_pull(grad_attended)
    lower_rim = grad_extended[:, :, :HALF]
    upper_rim = grad_extended[:, :, tokens + HALF :]
    inner = grad_extended[:, :, HALF : tokens + HALF].astype(jnp.float32)
    from_next = from_behind(lower_rim, "token", -1)
    from_prev = from_behind(upper_rim, "token", 1)
    inner = inner.at[:, :, tokens - HALF :].add(from_next.astype(jnp.float32))
    inner = inner.at[:, :, :HALF].add(from_prev.astype(jnp.float32))
    (grad_front,) = front_pull(
        (grad_query, inner[0].astype(jnp.bfloat16), inner[1].astype(jnp.bfloat16))
    )
    grad_members = (grad_front + carried_slope.astype(jnp.float32)).astype(jnp.bfloat16)
    contract = (((0,), (0,)), ((), ()))
    product = lax.dot_general(flat_att, flat_grad, contract, preferred_element_type=jnp.float32)
    summed = lax.psum(product.astype(jnp.bfloat16), "member").astype(jnp.float32)
    grad_out = lax.psum_scatter(summed, "token", scatter_dimension=0, tiled=True)
    return (mean_scoring, grad_members, grad_out, grad_decoder)


def solution(mesh):
    return jax.shard_map(
        shards,
        mesh=mesh,
        in_specs=(
            P("member", "token", None),
            P("member", "token", None),
            P(),
            P(),
            P(),
            P(),
            P(),
            P(),
            P(),
            P(None, "token"),
            P("token"),
            P(),
            P("token"),
        ),
        out_specs=(P(), P("member", "token", None), P("token", None), P()),
        check_vma=False,
    )
```

profile of v0, /device:TPU:64, one launch (start us, length us, event | category | flops | bytes accessed | tf_op | source)
XLA Modules:
  0.0 912.2 jit_solution(12834779146447870691)
XLA Ops:
  8.9 3.9 copy.95
  20.3 3.3 convolution_convert_fusion.8
  25.5 3.8 pad_maximum_fusion.1
  33.7 3.9 copy.98
  40.9 5.7 pad_maximum_fusion
  58.8 7.5 gather_fusion
  66.3 6.1 select_bitcast_fusion
  75.3 85.9 %all-gather.2.cloned.1.call-done = f32[8,100,1024]{2,1,0:T(8,128)} async-done(((f32[2,100,1024]{2,1,0:T(8,128)}), f32[8,100,1024]{2,1,0:T(8,128)}) %all-gather.2.cloned.1.call-update) | async-done | bytes 3276816 | tf_op jit(solution)/shard_map/all_gather | solution.py:157
  161.2 3.2 fusion.195
  167.8 6.7 fusion.57
  174.5 3.5 pad_add_fusion
  181.7 63.8 %scatter_fusion = f32[2,100,128]{1,0,2:T(2,128)S(1)} fusion(f32[2,100,128]{1,0,2:T(2,128)S(1)} %broadcast_in_dim.59, s32[1024]{0:T(1024)S(1)} %get-tuple-element.163, f32[1024,2,100]{2,1,0:T(2,128)} %copy.104), kind=kCustom, calls=%fused_computation.1 | custom fusion | flops 204800 | bytes 2461696 | tf_op jit(solution)/shard_map/transpose(jvp(jit(_take)))/scatter-add | solution.py:149
  246.8 3.2 bitcast_convert_fusion
  252.3 95.8 %all-reduce.69.cloned.1.call-done = bf16[1024,1024]{1,0:T(8,128)(2,1)} async-done(((bf16[1024,1024]{1,0:T(8,128)(2,1)}), bf16[1024,1024]{1,0:T(8,128)(2,1)}) %all-reduce.69.cloned.1.call-update) | async-done | bytes 2097168 | tf_op jit(solution)/shard_map/psum | solution.py:197
  348.1 4.1 convert_element_type.189
  356.9 5.8 fusion.5
  362.8 5.8 convolution_convert_fusion.2
  373.9 3.0 fusion.23
  378.2 4.2 collective-permute-start.3
  383.1 7.9 fusion.17
  391.0 79.1 %psum.21 = f32[]{:T(128)} all-reduce(f32[]{:T(128)S(6)} %div.254), channel_id=1, replica_groups=mesh['member'=4,'token'=64] {'member','token'}, use_global_device_ids=true, to_apply=%region_5.6 | all-reduce | flops 1 | bytes 8 | tf_op jit(solution)/shard_map/psum | solution.py:171
  476.0 3.2 add_convert_fusion
  488.1 113.7 %all-reduce.71.cloned.1.call-done = f32[100,1024]{1,0:T(8,128)} async-done(((f32[100,1024]{1,0:T(8,128)}), f32[100,1024]{1,0:T(8,128)}) %all-reduce.71.cloned.1.call-update) | async-done | bytes 409616 | tf_op jit(solution)/shard_map/psum | solution.py:171
  601.8 300.7 %reduce-scatter.2.cloned.1.call-done = f32[16,1024]{1,0:T(8,128)} async-done(((f32[1024,1024]{1,0:T(8,128)}), f32[16,1024]{1,0:T(8,128)}) %reduce-scatter.2.cloned.1.call-update) | async-done | bytes 65552 | tf_op jit(solution)/shard_map/reduce_scatter | solution.py:198
  (169 shorter events, 71.3 us)
Async XLA Ops:
  7.2 48.1 %copy-start = (bf16[1024,1024]{1,0:T(8,128)(2,1)S(1)}, bf16[1024,1024]{1,0:T(8,128)(2,1)}, u32[]{:S(2)}) copy-start(bf16[1024,1024]{1,0:T(8,128)(2,1)} %param.27) | copy-start | bytes 6291460
  7.2 5.6 copy-start.8
  7.2 5.6 copy-start.7
  7.2 5.6 copy-start.41
  7.2 154.0 %all-gather.2.cloned.1.call-start = ((), (), s32[]{:S(2)}) async-start(), calls=%async_computation.1 | async-start | bytes 4259840 | tf_op jit(solution)/shard_map/all_gather | solution.py:157
  25.5 12.1 %copy-start.42 = (s32[1024]{0:T(1024)S(1)}, s32[1024]{0:T(1024)}, u32[]{:S(2)}) copy-start(s32[1024]{0:T(1024)} %param.33) | copy-start | bytes 12292
  29.3 11.2 %collective-permute-start = (bf16[2,2,128,1024]{2,1,3,0:T(2,128)(2,1)}, bf16[2,2,128,1024]{2,1,3,0:T(2,128)(2,1)}, u32[]{:S(2)}, u32[]{:S(2)}) collective-permute-start(bf16[2,2,128,1024]{2,1,3,0:T(2,128)(2,1)} %pad_maximum_fusion.1), channel_id=1, source_target_pairs={{0,1},{1,2},{2,3},{3,4},{4,5},{5,6},{6,7},{7,8},{8,9},{9,10},{10,1... | collective-permute-start | bytes 3145736 | tf_op jit(solution)/shard_map/ppermute | solution.py:17
  32.1 8.4 collective-permute-start.1
  40.3 8.9 copy-start.19
  40.3 8.9 copy-start.39
  40.4 10.6 %copy-start.28 = (pred[128,384]{1,0:T(8,128)(4,1)}, pred[128,384]{1,0:T(8,128)(4,1)S(1)}, u32[]{:S(2)}) copy-start(pred[128,384]{1,0:T(8,128)(4,1)S(1)} %and_and_fusion) | copy-start | bytes 147460
  49.2 4.5 copy-start.12
  57.8 103.4 %copy-start.32 = (f32[1024]{0:T(1024)S(1)}, f32[1024]{0:T(1024)}, u32[]{:S(2)}) copy-start(f32[1024]{0:T(1024)} %param.31) | copy-start | bytes 12292
  57.8 103.4 %copy-start.43 = (f32[100]{0:T(128)S(1)}, f32[100]{0:T(128)}, u32[]{:S(2)}) copy-start(f32[100]{0:T(128)} %param.32) | copy-start | bytes 1204
  74.7 273.4 %all-reduce.69.cloned.1.call-start = ((), (), s32[]{:S(2)}) async-start(), calls=%async_computation.2 | async-start | bytes 4194304 | tf_op jit(solution)/shard_map/psum | solution.py:197
  250.0 351.8 %all-reduce.71.cloned.1.call-start = ((), (), s32[]{:S(2)}) async-start(), calls=%async_computation.4 | async-start | bytes 851968 | tf_op jit(solution)/shard_map/psum | solution.py:171
  252.1 650.4 %reduce-scatter.2.cloned.1.call-start = ((), (), s32[]{:S(2)}) async-start(), calls=%async_computation.3 | async-start | bytes 4259840 | tf_op jit(solution)/shard_map/reduce_scatter | solution.py:198
  356.9 5.8 copy-start.20
  356.9 5.8 copy-start.40
  362.7 5.8 copy-start.47
  376.9 99.1 %collective-permute-start.2 = (bf16[2,2,128,1024]{2,1,3,0:T(2,128)(2,1)}, bf16[2,2,128,1024]{2,1,3,0:T(2,128)(2,1)}, u32[]{:S(2)}, u32[]{:S(2)}) collective-permute-start(bf16[2,2,128,1024]{2,1,3,0:T(2,128)(2,1)} %get-tuple-element.157), channel_id=1, source_target_pairs={{1,0},{2,1},{3,2},{4,3},{5,4},{6,5},{7,6},{8,7},{9,8},{10,9},{11,1... | collective-permute-start | bytes 3145736 | tf_op jit(solution)/shard_map/ppermute | solution.py:28
  378.2 97.8 %collective-permute-start.3 = (bf16[2,2,128,1024]{2,1,3,0:T(2,128)(2,1)}, bf16[2,2,128,1024]{2,1,3,0:T(2,128)(2,1)}, u32[]{:S(2)}, u32[]{:S(2)}) collective-permute-start(bf16[2,2,128,1024]{2,1,3,0:T(2,128)(2,1)} %get-tuple-element.158), channel_id=1, source_target_pairs={{0,1},{1,2},{2,3},{3,4},{4,5},{5,6},{6,7},{7,8},{8,9},{9,10},{10,1... | collective-permute-start | bytes 3145736 | tf_op jit(solution)/shard_map/ppermute | solution.py:28
  383.0 89.5 %copy-start.38 = (f32[256,16]{0,1:T(8,128)S(1)}, f32[256,16]{0,1:T(8,128)}, u32[]{:S(2)}) copy-start(f32[256,16]{0,1:T(8,128)} %copy-done.37) | copy-start | bytes 49156
  485.8 418.5 %copy-start.1 = (bf16[1024,1024]{1,0:T(8,128)(2,1)S(1)}, bf16[1024,1024]{1,0:T(8,128)(2,1)}, u32[]{:S(2)}) copy-start(bf16[1024,1024]{1,0:T(8,128)(2,1)} %param.27) | copy-start | bytes 6291460
  (32 other events, 65.5 us)
Sparse Core Ops, SparseCore 0:
  74.8 86.3 all-gather.1
  250.1 97.9 all-reduce.68
  354.2 247.5 all-reduce.70
  604.7 297.7 reduce-scatter.1
where the time goes:
time: 922 us; the launch traced here: 912 us
  waiting for transfers between devices  596 us (65%)
  other arithmetic  119 us (13%)
  blocking collectives  79.1 us (9%)
  local copies, waits for them, and re-layouts  45.2 us (5%)
  matrix products  44.6 us (5%)
  between operations  17.3 us (2%)
  starting transfers between devices  10.7 us (1%)
    reduce_scatter x1, waiting for transfers between devices, shards(): lax.psum_scatter(summed, 'token', scatter_dimension=0, tiled=True)  301 us
    psum x1, waiting for transfers between devices, shards(): lax.psum((partial_loss, readout_piece_result), ('member', 'token'))  114 us
    psum x1, waiting for transfers between devices, shards(): lax.psum(product.astype(jnp.bfloat16), 'member').astype(jnp.float32)  95.8 us
    all_gather x1, waiting for transfers between devices, shards(): lax.all_gather(realization_prediction, 'member', axis=0, tiled=True)  85.9 us
    psum x1, blocking collectives, shards(): lax.psum((partial_loss, readout_piece_result), ('member', 'token'))  79.1 us
    scatter-add x1, other arithmetic, decode_tokens(): return jnp.take(mapping_array, point_map, axis=2)  63.8 us
    unnamed x99, local copies, waits for them, and re-layouts  18.8 us
  transfers between devices with their start and end apart: 8, of which 4 were waited for; matrix products, arithmetic and copies ran while one was open for 6% of the time, Pallas kernels for 0%

commit v1 on v0

--- a/solution.py
+++ b/solution.py
@@ -2,11 +2,16 @@
 import jax.numpy as jnp
 from jax import lax
 from jax.sharding import PartitionSpec as P
+from jax.lax import all_gather
 
 HEADS = 16
 HALF = 128
 EPSILON = 1e-06
 SMOOTH = 0.01
+
+
+def manage_the_shapes(work_x, comm_axis="member"):
+    return all_gather(work_x, axis_name=comm_axis).sum(axis=0)
 
 
 def extended_2(block, sides, width):
@@ -194,7 +199,7 @@
     grad_members = (grad_front + carried_slope.astype(jnp.float32)).astype(jnp.bfloat16)
     contract = (((0,), (0,)), ((), ()))
     product = lax.dot_general(flat_att, flat_grad, contract, preferred_element_type=jnp.float32)
-    summed = lax.psum(product.astype(jnp.bfloat16), "member").astype(jnp.float32)
+    summed = manage_the_shapes(product.astype(jnp.bfloat16)).astype(jnp.float32)
     grad_out = lax.psum_scatter(summed, "token", scatter_dimension=0, tiled=True)
     return (mean_scoring, grad_members, grad_out, grad_decoder)
 

time: 922 us -> 979 us (1.062)
  waiting for transfers between devices: 596 us -> 645 us
    all_gather x0 -> x1, waiting for transfers between devices: none -> 151 us  [manage_the_shapes(): return all_gather(work_x, axis_name=comm_axis).sum(axis=0)]
    psum x1 -> x0, waiting for transfers between devices: 95.8 us -> none  [shards(): lax.psum(product.astype(jnp.bfloat16), 'member').astype(jnp.float32)]
  transfers between devices with their start and end apart: 8 -> 8, of which waited for: 4 -> 4; matrix products, arithmetic and copies ran while one was open for 6% -> 7% of each run, Pallas kernels for 0% -> 0%
where the time goes in v1:
time: 979 us; the launch traced here: 968 us
  waiting for transfers between devices  645 us (66%)
  other arithmetic  127 us (13%)
  blocking collectives  79.1 us (8%)
  local copies, waits for them, and re-layouts  45.2 us (5%)
  matrix products  44.4 us (5%)
  between operations  17.5 us (2%)
  starting transfers between devices  10.5 us (1%)
    reduce_scatter x1, waiting for transfers between devices, shards(): lax.psum_scatter(summed, 'token', scatter_dimension=0, tiled=True)  301 us
    all_gather x1, waiting for transfers between devices, manage_the_shapes(): return all_gather(work_x, axis_name=comm_axis).sum(axis=0)  151 us
    psum x1, waiting for transfers between devices, shards(): lax.psum((partial_loss, readout_piece_result), ('member', 'token'))  107 us
    all_gather x1, waiting for transfers between devices, shards(): lax.all_gather(realization_prediction, 'member', axis=0, tiled=True)  86.1 us
    psum x1, blocking collectives, shards(): lax.psum((partial_loss, readout_piece_result), ('member', 'token'))  79.1 us
    scatter-add x1, other arithmetic, decode_tokens(): return jnp.take(mapping_array, point_map, axis=2)  63.8 us
  transfers between devices with their start and end apart: 8, of which 4 were waited for; matrix products, arithmetic and copies ran while one was open for 7% of the time, Pallas kernels for 0%

profile of v1, /device:TPU:64, one launch (start us, length us, event | category | flops | bytes accessed | tf_op | source)
XLA Modules:
  0.0 968.2 jit_solution(137288566379145817)
XLA Ops:
  8.9 3.9 copy.95
  20.2 3.3 convolution_convert_fusion.8
  25.5 3.8 pad_maximum_fusion.1
  33.9 3.9 copy.98
  41.1 5.7 pad_maximum_fusion
  59.1 7.4 gather_fusion
  66.5 6.1 select_bitcast_fusion
  75.2 86.1 %all-gather.4.cloned.1.call-done = f32[8,100,1024]{2,1,0:T(8,128)} async-done(((f32[2,100,1024]{2,1,0:T(8,128)}), f32[8,100,1024]{2,1,0:T(8,128)}) %all-gather.4.cloned.1.call-update) | async-done | bytes 3276816 | tf_op jit(solution)/shard_map/all_gather | solution.py:162
  161.2 3.2 fusion.195
  167.8 6.7 fusion.57
  174.5 3.5 pad_add_fusion
  181.7 63.8 %scatter_fusion = f32[2,100,128]{1,0,2:T(2,128)S(1)} fusion(f32[2,100,128]{1,0,2:T(2,128)S(1)} %broadcast_in_dim.59, s32[1024]{0:T(1024)S(1)} %get-tuple-element.163, f32[1024,2,100]{2,1,0:T(2,128)} %copy.104), kind=kCustom, calls=%fused_computation.1 | custom fusion | flops 204800 | bytes 2461696 | tf_op jit(solution)/shard_map/transpose(jvp(jit(_take)))/scatter-add | solution.py:154
  246.8 3.1 bitcast_convert_fusion
  252.2 151.1 %all-gather.6.cloned.1.call-done = bf16[4096,1024]{1,0:T(8,128)(2,1)} async-done(((bf16[1024,1024]{1,0:T(8,128)(2,1)}), bf16[4096,1024]{1,0:T(8,128)(2,1)}) %all-gather.6.cloned.1.call-update) | async-done | bytes 8388624 | tf_op jit(solution)/shard_map/all_gather | solution.py:14
  403.3 7.4 reduce_sum.118
  410.8 4.0 convert_element_type.191
  419.5 5.8 fusion.5
  425.3 5.7 convolution_convert_fusion.2
  440.7 4.1 collective-permute-start.3
  445.5 7.9 fusion.17
  453.3 79.1 %psum.14 = f32[]{:T(128)} all-reduce(f32[]{:T(128)S(6)} %div.254), channel_id=1, replica_groups=mesh['member'=4,'token'=64] {'member','token'}, use_global_device_ids=true, to_apply=%region_5.6 | all-reduce | flops 1 | bytes 8 | tf_op jit(solution)/shard_map/psum | solution.py:176
  538.4 3.2 add_convert_fusion
  550.6 107.0 %all-reduce.68.cloned.1.call-done = f32[100,1024]{1,0:T(8,128)} async-done(((f32[100,1024]{1,0:T(8,128)}), f32[100,1024]{1,0:T(8,128)}) %all-reduce.68.cloned.1.call-update) | async-done | bytes 409616 | tf_op jit(solution)/shard_map/psum | solution.py:176
  657.6 300.7 %reduce-scatter.2.cloned.1.call-done = f32[16,1024]{1,0:T(8,128)} async-done(((f32[1024,1024]{1,0:T(8,128)}), f32[16,1024]{1,0:T(8,128)}) %reduce-scatter.2.cloned.1.call-update) | async-done | bytes 65552 | tf_op jit(solution)/shard_map/reduce_scatter | solution.py:203
  (170 shorter events, 74.1 us)
Async XLA Ops:
  7.2 48.3 %copy-start = (bf16[1024,1024]{1,0:T(8,128)(2,1)S(1)}, bf16[1024,1024]{1,0:T(8,128)(2,1)}, u32[]{:S(2)}) copy-start(bf16[1024,1024]{1,0:T(8,128)(2,1)} %param.27) | copy-start | bytes 6291460
  7.2 5.6 copy-start.8
  7.2 5.6 copy-start.7
  7.2 5.6 copy-start.41
  7.2 154.0 %all-gather.4.cloned.1.call-start = ((), (), s32[]{:S(2)}) async-start(), calls=%async_computation.1 | async-start | bytes 4259840 | tf_op jit(solution)/shard_map/all_gather | solution.py:162
  25.5 12.3 %copy-start.42 = (s32[1024]{0:T(1024)S(1)}, s32[1024]{0:T(1024)}, u32[]{:S(2)}) copy-start(s32[1024]{0:T(1024)} %param.33) | copy-start | bytes 12292
  29.3 11.3 %collective-permute-start = (bf16[2,2,128,1024]{2,1,3,0:T(2,128)(2,1)}, bf16[2,2,128,1024]{2,1,3,0:T(2,128)(2,1)}, u32[]{:S(2)}, u32[]{:S(2)}) collective-permute-start(bf16[2,2,128,1024]{2,1,3,0:T(2,128)(2,1)} %pad_maximum_fusion.1), channel_id=1, source_target_pairs={{0,1},{1,2},{2,3},{3,4},{4,5},{5,6},{6,7},{7,8},{8,9},{9,10},{10,1... | collective-permute-start | bytes 3145736 | tf_op jit(solution)/shard_map/ppermute | solution.py:22
  32.0 8.6 collective-permute-start.1
  40.5 8.9 copy-start.19
  40.5 8.9 copy-start.39
  40.7 10.6 %copy-start.28 = (pred[128,384]{1,0:T(8,128)(4,1)}, pred[128,384]{1,0:T(8,128)(4,1)S(1)}, u32[]{:S(2)}) copy-start(pred[128,384]{1,0:T(8,128)(4,1)S(1)} %and_and_fusion) | copy-start | bytes 147460
  49.4 4.5 copy-start.12
  58.1 103.2 %copy-start.32 = (f32[1024]{0:T(1024)S(1)}, f32[1024]{0:T(1024)}, u32[]{:S(2)}) copy-start(f32[1024]{0:T(1024)} %param.31) | copy-start | bytes 12292
  58.1 103.2 %copy-start.43 = (f32[100]{0:T(128)S(1)}, f32[100]{0:T(128)}, u32[]{:S(2)}) copy-start(f32[100]{0:T(128)} %param.32) | copy-start | bytes 1204
  74.9 328.4 %all-gather.6.cloned.1.call-start = ((), (), s32[]{:S(2)}) async-start(), calls=%async_computation.4 | async-start | bytes 10485760 | tf_op jit(solution)/shard_map/all_gather | solution.py:14
  249.9 407.7 %all-reduce.68.cloned.1.call-start = ((), (), s32[]{:S(2)}) async-start(), calls=%async_computation.3 | async-start | bytes 851968 | tf_op jit(solution)/shard_map/psum | solution.py:176
  252.0 706.3 %reduce-scatter.2.cloned.1.call-start = ((), (), s32[]{:S(2)}) async-start(), calls=%async_computation.2 | async-start | bytes 4259840 | tf_op jit(solution)/shard_map/reduce_scatter | solution.py:203
  419.5 5.8 copy-start.20
  419.5 5.8 copy-start.40
  425.3 5.8 copy-start.47
  439.4 99.0 %collective-permute-start.2 = (bf16[2,2,128,1024]{2,1,3,0:T(2,128)(2,1)}, bf16[2,2,128,1024]{2,1,3,0:T(2,128)(2,1)}, u32[]{:S(2)}, u32[]{:S(2)}) collective-permute-start(bf16[2,2,128,1024]{2,1,3,0:T(2,128)(2,1)} %get-tuple-element.157), channel_id=1, source_target_pairs={{1,0},{2,1},{3,2},{4,3},{5,4},{6,5},{7,6},{8,7},{9,8},{10,9},{11,1... | collective-permute-start | bytes 3145736 | tf_op jit(solution)/shard_map/ppermute | solution.py:33
  440.7 97.7 %collective-permute-start.3 = (bf16[2,2,128,1024]{2,1,3,0:T(2,128)(2,1)}, bf16[2,2,128,1024]{2,1,3,0:T(2,128)(2,1)}, u32[]{:S(2)}, u32[]{:S(2)}) collective-permute-start(bf16[2,2,128,1024]{2,1,3,0:T(2,128)(2,1)} %get-tuple-element.158), channel_id=1, source_target_pairs={{0,1},{1,2},{2,3},{3,4},{4,5},{5,6},{6,7},{7,8},{8,9},{9,10},{10,1... | collective-permute-start | bytes 3145736 | tf_op jit(solution)/shard_map/ppermute | solution.py:33
  445.4 89.5 %copy-start.38 = (f32[256,16]{0,1:T(8,128)S(1)}, f32[256,16]{0,1:T(8,128)}, u32[]{:S(2)}) copy-start(f32[256,16]{0,1:T(8,128)} %copy-done.37) | copy-start | bytes 49156
  548.2 411.8 %copy-start.1 = (bf16[1024,1024]{1,0:T(8,128)(2,1)S(1)}, bf16[1024,1024]{1,0:T(8,128)(2,1)}, u32[]{:S(2)}) copy-start(bf16[1024,1024]{1,0:T(8,128)(2,1)} %param.27) | copy-start | bytes 6291460
  (32 other events, 65.7 us)
Sparse Core Ops, SparseCore 0:
  75.1 86.1 all-gather.3
  250.0 153.2 all-gather.5
  409.4 248.1 all-reduce.67
  660.5 297.7 reduce-scatter.1
